TPU v7x, 512 devices: a whole 4x8x8 slice. The times are simulated.
512 devices in a mesh: ens: 4 (over z_hi), lon: 32 (over z_lo, y, core), lat: 4 (over x).
Axes of the slice: x: 4, y: 8, z: 8 (z_hi: 4, z_lo: 2; z = z_hi * 2 + z_lo), core: 2. Of those that a mesh axis runs over, the one named last changes fastest.
Arguments:
- ocean_state: bfloat16 [4, 200, 32, 4096], P('ens', None, 'lat', 'lon'), may hold values from -6 to 6
- ocean_mask: int32 [32, 4096], P('lat', 'lon'), may hold values from 0 to 1, as said below
- dw_weight: float32 [200, 49], replicated, may hold values from -0.875 to 0.875
- norm_gain: float32 [200], replicated, may hold values from 0.1 to 1.9
- expand_weight: bfloat16 [200, 800], replicated, may hold values from -0.4375 to 0.4375
- reduce_weight: bfloat16 [800, 200], replicated, may hold values from -0.21875 to 0.21875
- cotangent: bfloat16 [4, 200, 32, 4096], P('ens', None, 'lat', 'lon'), may hold values from -6 to 6
Outputs:
- next_state: bfloat16 [4, 200, 32, 4096], P('ens', None, 'lat', 'lon')
- grad_depthwise: float32 [200, 49], replicated
- grad_gain: float32 [200], replicated
- grad_expand: float32 [200, 800], replicated
- grad_reduce: float32 [800, 200], replicated
Inputs may be any that keep to these rules, and one draw needn't show every extreme that they name: `ocean_mask`: the share of ocean cells differs from tile to tile of 8 x 128 cells, from about a third to nearly all.
All inputs are finite; a program needn't handle non-finite values.
Results may differ from a plain program's by a relative error of at most 0.0058.
Values may be sent and summed in bfloat16 or wider, within the bound.
No kernel may reach another device: no remote copies, remote signals or barrier semaphores. Data moves between devices by JAX's collectives and lax.ppermute only.
A program may use at most 64 MiB of HBM per device.

v0:
```python
import math
import jax
import jax.numpy as jnp
from jax import lax
from jax.sharding import PartitionSpec as P

KS = 7
norm_eps = 1e-06
root_half = 0.7071067811865476
gauss_norm = 0.3989422804014327


def with_halo(cells, sides, width):
    for axis, dim in sides:
        count = lax.axis_size(axis)
        head = lax.slice_in_dim(cells, 0, width, axis=dim)
        tail = lax.slice_in_dim(cells, cells.shape[dim] - width, cells.shape[dim], axis=dim)
        cells = jnp.concatenate(
            [
                lax.ppermute(tail, axis, [(i, (i + 1) % count) for i in range(count)]),
                cells,
                lax.ppermute(head, axis, [((i + 1) % count, i) for i in range(count)]),
            ],
            axis=dim,
        )
    return cells


def swapped(array, axis, stride):
    return lax.ppermute(array, axis, [(i, i ^ 1 << stride) for i in range(lax.axis_size(axis))])


def depthwise(padded, dw_weight, out_rows, out_cols):
    conv_sum = jnp.zeros((padded.shape[0], out_rows, out_cols), jnp.float32)
    for shift_a in range(KS):
        for shift_b in range(KS):
            tap_weight = dw_weight[:, shift_a * KS + shift_b][:, None, None]
            window = padded[:, shift_a : shift_a + out_rows, shift_b : shift_b + out_cols].astype(
                jnp.float32
            )
            conv_sum = conv_sum + tap_weight * window
    return conv_sum


def depthwise_grad(d_conv, padded, out_rows, out_cols):
    columns = []
    for shift_a in range(KS):
        for shift_b in range(KS):
            window = padded[:, shift_a : shift_a + out_rows, shift_b : shift_b + out_cols].astype(
                jnp.float32
            )
            columns.append(jnp.sum(d_conv * window, axis=(1, 2)))
    return jnp.stack(columns, axis=1)


def cell_pass(conv_blk, state_blk, cot_blk, mask_blk, norm_gain, expand_weight, reduce_weight):
    chan_mean = jnp.mean(conv_blk, axis=0, keepdims=True)
    centred = conv_blk - chan_mean
    chan_var = jnp.mean(centred * centred, axis=0, keepdims=True)
    inv_std = lax.rsqrt(chan_var + norm_eps)
    normed = centred * inv_std
    scaled = (normed * norm_gain[:, None]).astype(jnp.bfloat16)
    pre_act = jnp.dot(expand_weight.T, scaled, preferred_element_type=jnp.float32)
    normal_cdf = 0.5 * (1.0 + lax.erf(pre_act * root_half))
    normal_pdf = jnp.exp(-0.5 * pre_act * pre_act) * gauss_norm
    hidden = (pre_act * normal_cdf).astype(jnp.bfloat16)
    gelu_slope = normal_cdf + pre_act * normal_pdf
    branch = jnp.dot(reduce_weight.T, hidden, preferred_element_type=jnp.float32)
    out_blk = ((state_blk.astype(jnp.float32) + branch) * mask_blk[None, :]).astype(jnp.bfloat16)
    grad_reduce = jnp.dot(hidden, cot_blk.T, preferred_element_type=jnp.float32)
    d_hidden = jnp.dot(reduce_weight, cot_blk, preferred_element_type=jnp.float32)
    d_pre = (d_hidden * gelu_slope).astype(jnp.bfloat16)
    grad_expand = jnp.dot(scaled, d_pre.T, preferred_element_type=jnp.float32)
    d_scaled = jnp.dot(expand_weight, d_pre, preferred_element_type=jnp.float32)
    grad_gain = jnp.sum(d_scaled * normed, axis=1)
    d_normed = d_scaled * norm_gain[:, None]
    d_conv = inv_std * (
        d_normed
        - jnp.mean(d_normed, axis=0, keepdims=True)
        - normed * jnp.mean(d_normed * normed, axis=0, keepdims=True)
    )
    return (out_blk, d_conv, grad_expand, grad_reduce, grad_gain)


def body(ocean_state, ocean_mask, dw_weight, norm_gain, expand_weight, reduce_weight, cotangent):
    state_tile = ocean_state[0]
    channels = state_tile.shape[0]
    tile_rows = state_tile.shape[1]
    tile_cols = state_tile.shape[2]
    margin = KS // 2
    mask_bf = ocean_mask.astype(jnp.bfloat16)
    masked = state_tile * mask_bf[None]
    padded = with_halo(masked, (("lon", 2), ("lat", 1)), margin)
    lat_now = lax.axis_index("lat")
    lat_count = lax.axis_size("lat")
    lon_count = lax.axis_size("lon")
    top_strip = padded[:, tile_rows : tile_rows + margin, :][:, ::-1, ::-1]
    mirrored = top_strip
    for bit_number in range(lon_count.bit_length() - 1):
        mirrored = swapped(mirrored, "lon", bit_number)
    north_rows = jnp.where(lat_now == lat_count - 1, mirrored, padded[:, tile_rows + margin :, :])
    south_rows = jnp.where(lat_now == 0, jnp.zeros_like(top_strip), padded[:, :margin, :])
    padded = jnp.concatenate(
        [south_rows, padded[:, margin : tile_rows + margin, :], north_rows], axis=1
    )
    conv_out = depthwise(padded, dw_weight, tile_rows, tile_cols)
    cell_count = tile_rows * tile_cols
    cot_masked = (cotangent[0] * mask_bf[None]).reshape(channels, cell_count)
    out_flat, d_conv, grad_expand, grad_reduce, grad_gain = cell_pass(
        conv_out.reshape(channels, cell_count),
        state_tile.reshape(channels, cell_count),
        cot_masked,
        ocean_mask.astype(jnp.float32).reshape(cell_count),
        norm_gain,
        expand_weight,
        reduce_weight,
    )
    grad_depthwise = depthwise_grad(
        d_conv.reshape(channels, tile_rows, tile_cols), padded, tile_rows, tile_cols
    )
    grad_scale = 1.0 / math.sqrt(lax.axis_size("ens") * lat_count * lon_count * cell_count)
    grad_expand = grad_expand * grad_scale
    grad_reduce = grad_reduce * grad_scale
    grad_gain = grad_gain * grad_scale
    grad_depthwise = grad_depthwise * grad_scale
    grad_expand, grad_reduce, grad_gain, grad_depthwise = lax.psum(
        (grad_expand, grad_reduce, grad_gain, grad_depthwise), ("ens", "lon", "lat")
    )
    next_state = out_flat.reshape(channels, tile_rows, tile_cols)[None]
    return (next_state, grad_depthwise, grad_gain, grad_expand, grad_reduce)


def solution(mesh):
    return jax.shard_map(
        body,
        mesh=mesh,
        in_specs=(
            P("ens", None, "lat", "lon"),
            P("lat", "lon"),
            P(),
            P(),
            P(),
            P(),
            P("ens", None, "lat", "lon"),
        ),
        out_specs=(P("ens", None, "lat", "lon"), P(), P(), P(), P()),
        check_vma=False,
    )
```

profile of v0, /device:TPU:17, one launch (start us, length us, event | category | flops | bytes accessed | tf_op | source)
XLA Modules:
  0.0 393.7 jit_solution(8443036720947394535)
XLA Ops:
  7.2 0.0 copy-start
  7.2 0.0 all-reduce.4.cloned.1.call-start
  7.2 1.4 convert_bitcast_fusion
  8.6 1.3 copy.12
  9.9 0.2 bitcast_multiply_fusion.2
  10.1 3.8 collective-permute-start
  13.9 1.9 collective-permute-start.1
  15.8 0.0 collective-permute-done
  15.8 3.1 collective-permute-done.1
  18.9 0.1 pad_maximum_fusion.3
  19.0 1.0 rev.3
  20.1 1.9 collective-permute-start.3
  22.0 1.4 collective-permute-done.3
  23.4 5.6 %collective-permute-start.4 = (bf16[200,3,134]{0,2,1:T(8,128)(2,1)S(1)}, bf16[200,3,134]{0,2,1:T(8,128)(2,1)S(1)}, u32[]{:S(2)}, u32[]{:S(2)}) collective-permute-start(bf16[200,3,134]{0,2,1:T(8,128)(2,1)S(1)} %collective-permute-done.3), channel_id=1, source_target_pairs={{0,8},{4,12},{8,0},{12,4},{16,24},{20,28},{24,16},{28,20},{32,40},... | collective-permute-start | bytes 482408 | tf_op jit(solution)/shard_map/ppermute | solution.py:30
  29.1 5.4 %collective-permute-done.4 = bf16[200,3,134]{0,2,1:T(8,128)(2,1)S(1)} collective-permute-done((bf16[200,3,134]{0,2,1:T(8,128)(2,1)S(1)}, bf16[200,3,134]{0,2,1:T(8,128)(2,1)S(1)}, u32[]{:S(2)}, u32[]{:S(2)}) %collective-permute-start.4) | collective-permute-done | bytes 160832 | tf_op jit(solution)/shard_map/ppermute | solution.py:30
  34.4 5.2 %collective-permute-start.5 = (bf16[200,3,134]{0,2,1:T(8,128)(2,1)S(1)}, bf16[200,3,134]{0,2,1:T(8,128)(2,1)S(1)}, u32[]{:S(2)}, u32[]{:S(2)}) collective-permute-start(bf16[200,3,134]{0,2,1:T(8,128)(2,1)S(1)} %collective-permute-done.4), channel_id=1, source_target_pairs={{0,16},{4,20},{8,24},{12,28},{16,0},{20,4},{24,8},{28,12},{32,48},... | collective-permute-start | bytes 482408 | tf_op jit(solution)/shard_map/ppermute | solution.py:30
  39.6 1.9 collective-permute-start.2
  41.5 7.3 %collective-permute-done.5 = bf16[200,3,134]{0,2,1:T(8,128)(2,1)S(1)} collective-permute-done((bf16[200,3,134]{0,2,1:T(8,128)(2,1)S(1)}, bf16[200,3,134]{0,2,1:T(8,128)(2,1)S(1)}, u32[]{:S(2)}, u32[]{:S(2)}) %collective-permute-start.5) | collective-permute-done | bytes 160832 | tf_op jit(solution)/shard_map/ppermute | solution.py:30
  48.9 1.9 collective-permute-start.6
  50.8 2.7 collective-permute-start.8
  53.5 9.6 %collective-permute-done.6 = bf16[200,3,134]{0,2,1:T(8,128)(2,1)S(1)} collective-permute-done((bf16[200,3,134]{0,2,1:T(8,128)(2,1)S(1)}, bf16[200,3,134]{0,2,1:T(8,128)(2,1)S(1)}, u32[]{:S(2)}, u32[]{:S(2)}) %collective-permute-start.6) | collective-permute-done | bytes 160832 | tf_op jit(solution)/shard_map/ppermute | solution.py:30
  63.1 1.9 collective-permute-start.7
  65.1 0.0 collective-permute-done.2
  65.1 0.0 collective-permute-done.8
  65.1 5.1 %collective-permute-done.7 = bf16[200,3,134]{0,2,1:T(8,128)(2,1)S(1)} collective-permute-done((bf16[200,3,134]{0,2,1:T(8,128)(2,1)S(1)}, bf16[200,3,134]{0,2,1:T(8,128)(2,1)S(1)}, u32[]{:S(2)}, u32[]{:S(2)}) %collective-permute-start.7) | collective-permute-done | bytes 160832 | tf_op jit(solution)/shard_map/ppermute | solution.py:30
  70.3 0.2 maximum_maximum_fusion
  70.5 8.3 %fusion.118 = (f32[8,128]{1,0:T(8,128)S(1)}, f32[200,8,128]{0,2,1:T(8,128)S(1)}) fusion(bf16[200,11,134]{0,2,1:T(8,128)(2,1)S(1)} %get-tuple-element.77, f32[200]{0:T(256)S(1)} %bitcast.303, f32[200]{0:T(256)S(1)} %bitcast.304, f32[200]{0:T(256)S(1)} %bitcast.257, f32[200]{0:T(256)S(1)} %bitcast.258, f32[200]{0:T(256)S(1)} %bitcast.259, ...), kind=kLoop, calls=%fused_computation.252 | loop fusion | flops 33790976 | bytes 18494496 | tf_op jit(solution)/shard_map/reduce_sum | solution.py:57
  78.8 0.0 copy-start.8
  78.8 0.4 multiply_reduce_fusion
  79.2 0.6 copy-done.1
  79.8 1.5 copy.62
  81.3 0.0 copy-done
  81.3 0.0 copy-done.8
  81.3 0.0 copy-start.47
  81.4 0.0 copy-start.49
  81.4 2.2 fusion.9
  83.6 1.7 fusion.5
  85.3 1.7 convolution_multiply_fusion.1
  87.0 1.3 multiply_reduce_fusion.1
  88.3 0.0 copy-done.4
  88.3 1.3 multiply_reduce_fusion.2
  89.6 1.5 copy.63
  91.1 3.8 fusion.59
  94.9 3.8 fusion.109
  98.6 0.0 copy-done.48
  98.6 1.6 convolution_multiply_fusion
  100.3 0.0 all-reduce.4.cloned.1.call-update
  100.3 0.0 copy-start.5
  100.3 0.0 copy-start.33
  100.3 3.0 fusion.91
  103.4 0.0 copy-start.10
  103.4 0.0 copy-start.11
  103.4 0.0 copy-start.12
  103.4 0.0 copy-start.13
  103.4 0.0 copy-start.14
  103.4 0.0 copy-start.15
  103.7 0.0 copy-start.46
  103.7 1.6 fusion.13
  105.3 0.8 copy.65
  106.5 0.2 stack.199
  106.7 106.2 %all-reduce = (f32[200,49]{0,1:T(8,128)}, f32[200]{0:T(256)}) all-reduce(f32[200,49]{0,1:T(8,128)S(1)} %broadcast_multiply_fusion, f32[200]{0:T(256)S(1)} %broadcast_multiply_fusion.4), channel_id=1, replica_groups=mesh['ens'=4,'lon'=32,'lat'=4] {'ens','lon','lat'}, use_global_device_ids=true, to_apply=%region_53.54 | all-reduce | flops 10000 | bytes 80000 | tf_op jit(solution)/shard_map/psum | solution.py:126
  212.9 171.0 %all-reduce.4.cloned.1.call-done = (f32[200,800]{1,0:T(8,128)}, f32[800,200]{0,1:T(8,128)}) async-done(((f32[200,800]{1,0:T(8,128)}, f32[800,200]{0,1:T(8,128)}), (f32[200,800]{1,0:T(8,128)}, f32[800,200]{0,1:T(8,128)})) %all-reduce.4.cloned.1.call-update) | async-done | bytes 1280016 | tf_op jit(solution)/shard_map/psum | solution.py:126
  383.9 2.1 copy.74
  386.0 0.9 copy.75
  (93 shorter events, 0.3 us)
Async XLA Ops:
  7.2 74.2 %copy-start = (bf16[200,800]{1,0:T(8,128)(2,1)S(1)}, bf16[200,800]{1,0:T(8,128)(2,1)}, u32[]{:S(2)}) copy-start(bf16[200,800]{1,0:T(8,128)(2,1)} %param.11) | copy-start | bytes 960004
  7.2 376.7 %all-reduce.4.cloned.1.call-start = ((), (), s32[]{:S(2)}) async-start(), calls=%async_computation | async-start | bytes 2867200 | tf_op jit(solution)/shard_map/psum | solution.py:126
  8.6 20.4 %copy-start.7 = (f32[200,49]{0,1:T(8,128)S(1)}, f32[200,49]{0,1:T(8,128)}, u32[]{:S(2)}) copy-start(f32[200,49]{0,1:T(8,128)} %param.9) | copy-start | bytes 117604
  10.1 5.7 %collective-permute-start = (bf16[200,8,3]{0,2,1:T(4,128)(2,1)S(1)}, bf16[200,8,3]{0,2,1:T(4,128)(2,1)S(1)}, u32[]{:S(2)}, u32[]{:S(2)}) collective-permute-start(bf16[200,8,3]{0,2,1:T(4,128)(2,1)S(1)} %get-tuple-element.80), channel_id=1, source_target_pairs={{0,4},{4,8},{8,12},{12,16},{16,20},{20,24},{24,28},{28,32},{32,36}... | collective-permute-start | bytes 28808 | tf_op jit(solution)/shard_map/ppermute | solution.py:20
  13.9 5.1 %collective-permute-start.1 = (bf16[200,8,3]{0,2,1:T(4,128)(2,1)S(1)}, bf16[200,8,3]{0,2,1:T(4,128)(2,1)S(1)}, u32[]{:S(2)}, u32[]{:S(2)}) collective-permute-start(bf16[200,8,3]{0,2,1:T(4,128)(2,1)S(1)} %get-tuple-element.81), channel_id=1, source_target_pairs={{4,0},{8,4},{12,8},{16,12},{20,16},{24,20},{28,24},{32,28},{36,32}... | collective-permute-start | bytes 28808 | tf_op jit(solution)/shard_map/ppermute | solution.py:22
  20.1 3.4 collective-permute-start.3
  23.4 11.0 %collective-permute-start.4 = (bf16[200,3,134]{0,2,1:T(8,128)(2,1)S(1)}, bf16[200,3,134]{0,2,1:T(8,128)(2,1)S(1)}, u32[]{:S(2)}, u32[]{:S(2)}) collective-permute-start(bf16[200,3,134]{0,2,1:T(8,128)(2,1)S(1)} %collective-permute-done.3), channel_id=1, source_target_pairs={{0,8},{4,12},{8,0},{12,4},{16,24},{20,28},{24,16},{28,20},{32,40},... | collective-permute-start | bytes 482408 | tf_op jit(solution)/shard_map/ppermute | solution.py:30
  34.4 14.5 %collective-permute-start.5 = (bf16[200,3,134]{0,2,1:T(8,128)(2,1)S(1)}, bf16[200,3,134]{0,2,1:T(8,128)(2,1)S(1)}, u32[]{:S(2)}, u32[]{:S(2)}) collective-permute-start(bf16[200,3,134]{0,2,1:T(8,128)(2,1)S(1)} %collective-permute-done.4), channel_id=1, source_target_pairs={{0,16},{4,20},{8,24},{12,28},{16,0},{20,4},{24,8},{28,12},{32,48},... | collective-permute-start | bytes 482408 | tf_op jit(solution)/shard_map/ppermute | solution.py:30
  39.6 25.5 %collective-permute-start.2 = (bf16[200,3,134]{0,2,1:T(8,128)(2,1)S(1)}, bf16[200,3,134]{0,2,1:T(8,128)(2,1)S(1)}, u32[]{:S(2)}, u32[]{:S(2)}) collective-permute-start(bf16[200,3,134]{0,2,1:T(8,128)(2,1)S(1)} %get-tuple-element.79), channel_id=1, source_target_pairs={{0,1},{1,2},{2,3},{3,0},{4,5},{5,6},{6,7},{7,4},{8,9},{9,10},{10,1... | collective-permute-start | bytes 482408 | tf_op jit(solution)/shard_map/ppermute | solution.py:20
  48.9 14.3 %collective-permute-start.6 = (bf16[200,3,134]{0,2,1:T(8,128)(2,1)S(1)}, bf16[200,3,134]{0,2,1:T(8,128)(2,1)S(1)}, u32[]{:S(2)}, u32[]{:S(2)}) collective-permute-start(bf16[200,3,134]{0,2,1:T(8,128)(2,1)S(1)} %collective-permute-done.5), channel_id=1, source_target_pairs={{0,32},{4,36},{8,40},{12,44},{16,48},{20,52},{24,56},{28,60},{32,0... | collective-permute-start | bytes 482408 | tf_op jit(solution)/shard_map/ppermute | solution.py:30
  50.8 14.3 %collective-permute-start.8 = (bf16[200,3,134]{0,2,1:T(8,128)(2,1)S(1)}, bf16[200,3,134]{0,2,1:T(8,128)(2,1)S(1)}, u32[]{:S(2)}, u32[]{:S(2)}) collective-permute-start(bf16[200,3,134]{0,2,1:T(8,128)(2,1)S(1)} %get-tuple-element.78), channel_id=1, source_target_pairs={{1,0},{2,1},{3,2},{0,3},{5,4},{6,5},{7,6},{4,7},{9,8},{10,9},{11,1... | collective-permute-start | bytes 482408 | tf_op jit(solution)/shard_map/ppermute | solution.py:22
  63.1 7.1 %collective-permute-start.7 = (bf16[200,3,134]{0,2,1:T(8,128)(2,1)S(1)}, bf16[200,3,134]{0,2,1:T(8,128)(2,1)S(1)}, u32[]{:S(2)}, u32[]{:S(2)}) collective-permute-start(bf16[200,3,134]{0,2,1:T(8,128)(2,1)S(1)} %collective-permute-done.6), channel_id=1, source_target_pairs={{0,64},{4,68},{8,72},{12,76},{16,80},{20,84},{24,88},{28,92},{32,9... | collective-permute-start | bytes 482408 | tf_op jit(solution)/shard_map/ppermute | solution.py:30
  78.8 1.0 copy-start.1
  78.8 2.5 copy-start.8
  81.3 2.2 copy-start.47
  81.4 2.2 copy-start.49
  87.0 1.4 copy-start.4
  94.8 3.8 copy-start.2
  94.8 3.8 copy-start.48
  100.3 3.1 copy-start.3
  100.3 3.1 copy-start.5
  100.3 3.1 copy-start.33
  103.4 2.8 copy-start.9
  103.4 2.8 copy-start.10
  103.4 2.8 copy-start.11
  103.4 2.8 copy-start.12
  103.4 2.8 copy-start.13
  103.4 2.8 copy-start.14
  103.4 2.8 copy-start.15
  103.4 2.8 copy-start.16
  103.5 2.8 copy-start.17
  103.5 2.8 copy-start.18
  103.5 2.8 copy-start.19
  103.5 2.8 copy-start.20
  103.5 2.8 copy-start.21
  103.5 2.8 copy-start.22
  103.5 2.8 copy-start.23
  103.5 2.8 copy-start.24
  103.5 2.8 copy-start.25
  103.5 2.8 copy-start.26
  103.6 2.8 copy-start.27
  103.6 2.8 copy-start.28
  103.6 2.8 copy-start.29
  103.6 2.8 copy-start.30
  103.6 2.8 copy-start.31
  103.6 2.8 copy-start.32
  103.6 2.8 copy-start.34
  103.6 2.8 copy-start.35
  103.6 2.8 copy-start.36
  103.6 2.8 copy-start.37
  103.7 2.8 copy-start.38
  103.7 2.8 copy-start.39
  103.7 2.8 copy-start.40
  103.7 2.8 copy-start.41
  103.7 2.8 copy-start.42
  103.7 2.8 copy-start.43
  103.7 2.8 copy-start.44
  103.7 2.8 copy-start.45
  103.7 2.9 copy-start.46
  383.9 2.1 copy-start.6
Sparse Core Ops, SparseCore 0:
  100.4 283.4 all-reduce.3
where the time goes:
time: 394 us
  waiting for transfers between devices  203 us (52%)
  blocking collectives  106 us (27%)
  starting transfers between devices  26.9 us (7%)
  other arithmetic  22.5 us (6%)
  between operations  14.9 us (4%)
  matrix products  10.2 us (3%)
  local copies, waits for them, and re-layouts  10.1 us (3%)
    psum x1, waiting for transfers between devices, body(): lax.psum((grad_expand, grad_reduce, grad_gain, grad_depthwise), ('ens', '...  171 us
    psum x1, blocking collectives, body(): lax.psum((grad_expand, grad_reduce, grad_gain, grad_depthwise), ('ens', '...  106 us
    ppermute x5, waiting for transfers between devices, swapped(): lax.ppermute(array, axis, [(i, i ^ 1 << stride) for i in range(lax.axis_s...  28.8 us
    ppermute x5, starting transfers between devices, swapped(): lax.ppermute(array, axis, [(i, i ^ 1 << stride) for i in range(lax.axis_s...  16.5 us
    reduce_sum x4, other arithmetic, depthwise_grad(): columns.append(jnp.sum(d_conv * window, axis=(1, 2)))  11.9 us
    reduce_sum x1, other arithmetic, cell_pass(): chan_mean = jnp.mean(conv_blk, axis=0, keepdims=True)  8.28 us
  transfers between devices with their start and end apart: 10, of which 7 were waited for; matrix products, arithmetic and copies ran while one was open for 1% of the time, Pallas kernels for 0%

commit v1 on v0

--- a/solution.py
+++ b/solution.py
@@ -124,7 +124,7 @@
     grad_gain = grad_gain * grad_scale
     grad_depthwise = grad_depthwise * grad_scale
     grad_expand, grad_reduce, grad_gain, grad_depthwise = lax.psum(
-        (grad_expand, grad_reduce, grad_gain, grad_depthwise), ("ens", "lon", "lat")
+        lax.psum((grad_expand, grad_reduce, grad_gain, grad_depthwise), "ens"), ("lon", "lat")
     )
     next_state = out_flat.reshape(channels, tile_rows, tile_cols)[None]
     return (next_state, grad_depthwise, grad_gain, grad_expand, grad_reduce)

time: 394 us -> 1240 us (3.15)
  the two profiles are of different devices: /device:TPU:17 before, /device:TPU:64 now
where the time goes in v1:
time: 1240 us
  waiting for transfers between devices  579 us (47%)
  blocking collectives  570 us (46%)
  starting transfers between devices  35.6 us (3%)
  other arithmetic  20 us (2%)
  between operations  14.4 us (1%)
    psum x1, blocking collectives, body(): lax.psum(lax.psum((grad_expand, grad_reduce, grad_gain, grad_depthwise),...  551 us
    psum x1, waiting for transfers between devices, body(): lax.psum(lax.psum((grad_expand, grad_reduce, grad_gain, grad_depthwise),...  473 us
    psum x1, waiting for transfers between devices, body(): lax.psum((grad_expand, grad_reduce, grad_gain, grad_depthwise), 'ens')  81.4 us
  transfers between devices with their start and end apart: 11, of which 8 were waited for; matrix products, arithmetic and copies ran while one was open for 1% of the time, Pallas kernels for 0%

profile of v1, /device:TPU:64, one launch (start us, length us, event | category | flops | bytes accessed | tf_op | source)
XLA Modules:
  0.0 1239.2 jit_solution(16610624705198293118)
XLA Ops:
  7.2 0.0 copy-start
  7.2 0.0 all-reduce.9.cloned.1.call-start
  7.2 0.8 convert_bitcast_fusion
  8.0 1.3 copy.12
  9.3 0.2 bitcast_multiply_fusion.2
  9.5 1.9 collective-permute-start
  11.4 5.8 collective-permute-start.1
  17.2 0.0 collective-permute-done
  17.2 1.4 collective-permute-done.1
  18.6 0.1 pad_maximum_fusion.3
  18.7 1.0 rev.3
  19.7 1.9 collective-permute-start.3
  21.7 1.4 collective-permute-done.3
  23.1 2.7 collective-permute-start.4
  25.8 0.0 copy-done.6
  25.8 6.4 collective-permute-done.4
  32.2 6.2 collective-permute-start.5
  38.4 3.4 collective-permute-start.2
  41.8 6.2 collective-permute-done.5
  47.9 7.4 collective-permute-start.6
  55.3 2.0 collective-permute-start.8
  57.3 5.7 collective-permute-done.6
  63.1 4.2 collective-permute-start.7
  67.3 0.0 collective-permute-done.2
  67.3 0.0 collective-permute-done.8
  67.3 4.2 collective-permute-done.7
  71.6 0.2 maximum_maximum_fusion
  71.8 8.3 fusion.118
  80.1 0.0 copy-start.1
  80.1 0.0 copy-start.7
  80.2 0.4 multiply_reduce_fusion
  80.5 0.6 copy-done.1
  81.1 1.5 copy.62
  82.7 0.0 copy-done
  82.7 0.0 copy-done.7
  82.7 0.0 copy-start.8
  82.7 0.0 copy-start.9
  82.7 0.9 fusion.9
  83.6 0.0 copy-start.2
  83.6 0.1 copy-done.8
  83.7 0.1 copy-done.9
  83.8 1.7 fusion.5
  85.5 1.7 convolution_multiply_fusion.1
  87.2 1.6 multiply_reduce_fusion.1
  88.8 0.0 copy-done.2
  88.8 1.6 convolution_multiply_fusion
  90.5 2.3 fusion.13
  92.8 0.8 copy.65
  93.6 0.0 copy-done.3
  93.6 1.3 multiply_reduce_fusion.2
  94.9 1.5 copy.63
  96.3 0.0 all-reduce.9.cloned.1.call-update
  96.4 0.2 all-reduce.7.cloned.1.call-start
  96.6 2.4 fusion.91
  99.0 3.2 fusion.59
  102.2 81.4 %all-reduce.9.cloned.1.call-done = (f32[200,800]{1,0:T(8,128)}, f32[800,200]{0,1:T(8,128)}) async-done(((f32[200,800]{1,0:T(8,128)}, f32[800,200]{0,1:T(8,128)}), (f32[200,800]{1,0:T(8,128)}, f32[800,200]{0,1:T(8,128)})) %all-reduce.9.cloned.1.call-update) | async-done | bytes 1280016 | tf_op jit(solution)/shard_map/psum | solution.py:127
  183.6 0.0 all-reduce.7.cloned.1.call-update
  183.6 3.2 fusion.109
  186.7 0.2 stack.199
  186.9 18.8 %all-reduce.2 = (f32[200,49]{0,1:T(8,128)S(1)}, f32[200]{0:T(256)S(1)}) all-reduce(f32[200,49]{0,1:T(8,128)S(1)} %broadcast_multiply_fusion, f32[200]{0:T(256)S(1)} %broadcast_multiply_fusion.4), channel_id=1, replica_groups=mesh['ens'=4,'lon'=32,'lat'=4] {'ens'}, use_global_device_ids=true, to_apply=%region_53.54 | all-reduce | flops 10000 | bytes 80000 | tf_op jit(solution)/shard_map/psum | solution.py:127
  205.7 551.1 %all-reduce = (f32[200,49]{0,1:T(8,128)}, f32[200]{0:T(256)}) all-reduce(f32[200,49]{0,1:T(8,128)S(1)} %get-tuple-element.72, f32[200]{0:T(256)S(1)} %get-tuple-element.73), channel_id=1, replica_groups=mesh['ens'=4,'lon'=32,'lat'=4] {'lon','lat'}, use_global_device_ids=true, to_apply=%region_54.55 | all-reduce | flops 10000 | bytes 80000 | tf_op jit(solution)/shard_map/psum | solution.py:126
  756.8 472.7 %all-reduce.7.cloned.1.call-done = (f32[200,800]{1,0:T(8,128)}, f32[800,200]{0,1:T(8,128)}) async-done(((f32[200,800]{1,0:T(8,128)}, f32[800,200]{0,1:T(8,128)}), (f32[200,800]{1,0:T(8,128)}, f32[800,200]{0,1:T(8,128)})) %all-reduce.7.cloned.1.call-update) | async-done | bytes 1280016 | tf_op jit(solution)/shard_map/psum | solution.py:126
  1229.4 2.1 copy.76
  1231.5 0.9 copy.77
  (17 shorter events, 0.2 us)
Async XLA Ops:
  7.2 75.5 %copy-start = (bf16[200,800]{1,0:T(8,128)(2,1)S(1)}, bf16[200,800]{1,0:T(8,128)(2,1)}, u32[]{:S(2)}) copy-start(bf16[200,800]{1,0:T(8,128)(2,1)} %param.11) | copy-start | bytes 960004
  7.2 176.4 %all-reduce.9.cloned.1.call-start = ((), (), s32[]{:S(2)}) async-start(), calls=%async_computation.1 | async-start | bytes 2867200 | tf_op jit(solution)/shard_map/psum | solution.py:127
  8.0 17.8 %copy-start.6 = (f32[200,49]{0,1:T(8,128)S(1)}, f32[200,49]{0,1:T(8,128)}, u32[]{:S(2)}) copy-start(f32[200,49]{0,1:T(8,128)} %param.9) | copy-start | bytes 117604
  9.5 7.7 collective-permute-start
  11.4 7.2 collective-permute-start.1
  19.7 3.4 collective-permute-start.3
  23.1 9.1 collective-permute-start.4
  32.2 15.8 %collective-permute-start.5 = (bf16[200,3,134]{0,2,1:T(8,128)(2,1)S(1)}, bf16[200,3,134]{0,2,1:T(8,128)(2,1)S(1)}, u32[]{:S(2)}, u32[]{:S(2)}) collective-permute-start(bf16[200,3,134]{0,2,1:T(8,128)(2,1)S(1)} %collective-permute-done.4), channel_id=1, source_target_pairs={{0,16},{4,20},{8,24},{12,28},{16,0},{20,4},{24,8},{28,12},{32,48},... | collective-permute-start | bytes 482408 | tf_op jit(solution)/shard_map/ppermute | solution.py:30
  38.4 28.9 %collective-permute-start.2 = (bf16[200,3,134]{0,2,1:T(8,128)(2,1)S(1)}, bf16[200,3,134]{0,2,1:T(8,128)(2,1)S(1)}, u32[]{:S(2)}, u32[]{:S(2)}) collective-permute-start(bf16[200,3,134]{0,2,1:T(8,128)(2,1)S(1)} %get-tuple-element.83), channel_id=1, source_target_pairs={{0,1},{1,2},{2,3},{3,0},{4,5},{5,6},{6,7},{7,4},{8,9},{9,10},{10,1... | collective-permute-start | bytes 482408 | tf_op jit(solution)/shard_map/ppermute | solution.py:20
  47.9 15.1 %collective-permute-start.6 = (bf16[200,3,134]{0,2,1:T(8,128)(2,1)S(1)}, bf16[200,3,134]{0,2,1:T(8,128)(2,1)S(1)}, u32[]{:S(2)}, u32[]{:S(2)}) collective-permute-start(bf16[200,3,134]{0,2,1:T(8,128)(2,1)S(1)} %collective-permute-done.5), channel_id=1, source_target_pairs={{0,32},{4,36},{8,40},{12,44},{16,48},{20,52},{24,56},{28,60},{32,0... | collective-permute-start | bytes 482408 | tf_op jit(solution)/shard_map/ppermute | solution.py:30
  55.3 12.0 collective-permute-start.8
  63.1 8.5 collective-permute-start.7
  80.1 1.0 copy-start.1
  80.1 2.5 copy-start.7
  82.7 1.0 copy-start.8
  82.7 1.1 copy-start.9
  83.6 5.2 copy-start.2
  90.4 3.1 copy-start.3
  90.4 3.1 copy-start.4
  96.4 1133.1 %all-reduce.7.cloned.1.call-start = ((), (), s32[]{:S(2)}) async-start(), calls=%async_computation | async-start | bytes 2867200 | tf_op jit(solution)/shard_map/psum | solution.py:126
  1229.4 2.1 copy-start.5
Sparse Core Ops, SparseCore 0:
  96.5 87.0 all-reduce.8
  186.5 1042.8 all-reduce.6
